TPU v7x, 32 devices: a whole 2x2x4 slice. The times are simulated.
32 devices in a mesh: groups: 2 (over y), pix: 4 (over z), sub: 2 (over x), inner: 2 (over core).
Axes of the slice: x: 2, y: 2, z: 4, core: 2. Of those that a mesh axis runs over, the one named last changes fastest.
Arguments:
- cube: bfloat16 [20480, 256], P(('groups', 'pix', 'sub', 'inner')), parts along dimension 0, may hold values from -70 to 70
Outputs:
- spectra: bfloat16 [256, 16, 1280], P(('pix', 'sub'), 'groups', 'inner'), parts along dimension 1
There are 2 independent parts, one for each index of `groups`. A program takes and returns all parts, laid end to end along the dimension named above; each array names one. Nothing has to cross between parts.
All inputs are finite; a program needn't handle non-finite values.
Results may differ from a plain program's by a relative error of at most 0.0067.
Values may be sent and summed in bfloat16 or wider, within the bound.
No kernel may reach another device: no remote copies, remote signals or barrier semaphores. Data moves between devices by JAX's collectives and lax.ppermute only.
A program may use at most 64 MiB of HBM per device.

v0:
```python
import math
import jax
import jax.numpy as jnp
from jax import lax
from jax.sharding import PartitionSpec as P

MODES = 32
ITERS = 4
VARIANT = "symbutterfly"


def matmul_high(left, right):
    return jnp.dot(left, right, precision=lax.Precision.HIGHEST)


def leading_modes(gram_matrix, width_count, sweeps):
    mode_basis = jnp.eye(gram_matrix.shape[0], width_count, dtype=jnp.float32)
    for iteration in range(sweeps):
        product = matmul_high(gram_matrix, mode_basis)
        cross_gram = matmul_high(product.T, product)
        lower_factor = jnp.linalg.cholesky(cross_gram)
        mode_basis = jax.scipy.linalg.solve_triangular(lower_factor, product.T, lower=True).T
    return mode_basis


def delay_table(channels):
    middle = channels // 2
    row_index = lax.broadcasted_iota(jnp.int32, (channels, channels), 0)
    col_index = lax.broadcasted_iota(jnp.int32, (channels, channels), 1)
    harmonic = jnp.where(row_index <= middle, row_index, row_index - middle)
    angles = (harmonic * col_index % channels).astype(jnp.float32) * (2.0 * math.pi / channels)
    values = jnp.where(row_index <= middle, jnp.cos(angles), jnp.sin(angles)) / math.sqrt(channels)
    return values.astype(jnp.bfloat16)


def steps_of(sizes):
    out = []
    for name, n in sizes:
        d = 1
        while d < n:
            out.append((name, n, d))
            d *= 2
    return out


def butterfly_sum(x, sizes):
    for name, n, d in steps_of(sizes):
        x = x + lax.ppermute(x, name, [(i, i ^ d) for i in range(n)])
    return x


def halving_sum(x, sizes):
    steps = steps_of(sizes)
    for name, n, d in steps:
        bit = lax.axis_index(name) // d % 2
        half = x.shape[0] // 2
        lo, hi = (x[:half], x[half:])
        send = jnp.where(bit == 0, hi, lo)
        keep = jnp.where(bit == 0, lo, hi)
        x = keep + lax.ppermute(send, name, [(i, i ^ d) for i in range(n)])
    for name, n, d in reversed(steps):
        bit = lax.axis_index(name) // d % 2
        other = lax.ppermute(x, name, [(i, i ^ d) for i in range(n)])
        x = jnp.where(bit == 0, jnp.concatenate([x, other]), jnp.concatenate([other, x]))
    return x


def make_local(sizes):

    def reduce(g):
        if VARIANT == "psum":
            return lax.psum(g, ("pix", "sub", "inner"))
        if VARIANT == "butterfly":
            return butterfly_sum(g, sizes)
        if VARIANT == "halving":
            return halving_sum(g, sizes)
        if VARIANT == "symbutterfly":
            h = g.shape[0] // 2
            packed = jnp.concatenate([g[:h, :h], g[:h, h:], g[h:, h:]], axis=0)
            packed = butterfly_sum(packed, sizes)
            a, b, d = (packed[:h], packed[h : 2 * h], packed[2 * h :])
            return jnp.concatenate([jnp.concatenate([a, b], 1), jnp.concatenate([b.T, d], 1)], 0)
        raise ValueError(VARIANT)

    def local(cube):
        pixels, channels = cube.shape
        pixel_count = pixels * lax.axis_size(("pix", "sub", "inner"))
        partial_gram = lax.dot_general(
            cube, cube, (((0,), (0,)), ((), ())), preferred_element_type=jnp.float32
        )
        gram_matrix = reduce(partial_gram)
        gram_matrix = gram_matrix / pixel_count
        mode_basis = leading_modes(gram_matrix, MODES, ITERS)
        modes_b = mode_basis.astype(jnp.bfloat16)
        amplitudes = jnp.dot(cube, modes_b, preferred_element_type=jnp.float32).astype(jnp.bfloat16)
        cleaned = (
            cube - jnp.dot(amplitudes, modes_b.T, preferred_element_type=jnp.float32)
        ).astype(jnp.bfloat16)
        table_b = delay_table(channels)
        coefficients = lax.dot_general(
            table_b, cleaned, (((1,), (1,)), ((), ())), preferred_element_type=jnp.float32
        ).astype(jnp.bfloat16)
        spectra = lax.all_to_all(
            coefficients[:, None, :], ("pix", "sub"), split_axis=0, concat_axis=1, tiled=True
        )
        return spectra

    return local


def solution(mesh):
    sizes = [(a, mesh.shape[a]) for a in ("inner", "sub", "pix")]
    return jax.shard_map(
        make_local(sizes),
        mesh=mesh,
        in_specs=(P(("groups", "pix", "sub", "inner"), None),),
        out_specs=P(("pix", "sub"), "groups", "inner"),
        check_vma=False,
    )
```

profile of v0, /device:TPU:0, one launch (start us, length us, event | category | flops | bytes accessed | tf_op | source)
XLA Modules:
  0.0 79.0 jit_solution(11939756387512066337)
XLA Ops:
  0.0 1.4 %fusion.49 = f32[256,256]{1,0:T(8,128)S(1)} fusion(bf16[640,256]{1,0:T(8,128)(2,1)} %param.4), kind=kOutput, calls=%fused_computation.78 | convolution fusion | flops 83886080 | bytes 589824 | tf_op jit(solution)/shard_map/dot_general | solution.py:88
  2.0 1.1 %collective-permute-done = f32[384,128]{1,0:T(8,128)S(1)} collective-permute-done((f32[384,128]{1,0:T(8,128)S(1)}, f32[384,128]{1,0:T(8,128)S(1)}, u32[]{:S(2)}, u32[]{:S(2)}) %collective-permute-start) | collective-permute-done | bytes 196640 | tf_op jit(solution)/shard_map/ppermute | solution.py:48
  3.1 2.9 %collective-permute-start.1 = (f32[384,128]{1,0:T(8,128)S(1)}, f32[384,128]{1,0:T(8,128)S(1)}, u32[]{:S(2)}, u32[]{:S(2)}) collective-permute-start(f32[384,128]{1,0:T(8,128)S(1)} %fusion.44), channel_id=1, source_target_pairs={{0,2},{2,0},{1,3},{3,1},{4,6},{6,4},{5,7},{7,5},{8,10},{10,8},{9,1... | collective-permute-start | bytes 589832 | tf_op jit(solution)/shard_map/ppermute | solution.py:48
  6.0 5.2 %collective-permute-done.1 = f32[384,128]{1,0:T(8,128)S(1)} collective-permute-done((f32[384,128]{1,0:T(8,128)S(1)}, f32[384,128]{1,0:T(8,128)S(1)}, u32[]{:S(2)}, u32[]{:S(2)}) %collective-permute-start.1) | collective-permute-done | bytes 196640 | tf_op jit(solution)/shard_map/ppermute | solution.py:48
  11.2 1.9 %collective-permute-start.2 = (f32[384,128]{1,0:T(8,128)S(1)}, f32[384,128]{1,0:T(8,128)S(1)}, u32[]{:S(2)}, u32[]{:S(2)}) collective-permute-start(f32[384,128]{1,0:T(8,128)S(1)} %add.30), channel_id=1, source_target_pairs={{0,4},{4,0},{8,12},{12,8},{1,5},{5,1},{9,13},{13,9},{2,6},{6,2},{1... | collective-permute-start | bytes 589832 | tf_op jit(solution)/shard_map/ppermute | solution.py:48
  13.1 4.5 %collective-permute-done.2 = f32[384,128]{1,0:T(8,128)S(1)} collective-permute-done((f32[384,128]{1,0:T(8,128)S(1)}, f32[384,128]{1,0:T(8,128)S(1)}, u32[]{:S(2)}, u32[]{:S(2)}) %collective-permute-start.2) | collective-permute-done | bytes 196640 | tf_op jit(solution)/shard_map/ppermute | solution.py:48
  17.7 2.6 %collective-permute-start.3 = (f32[384,128]{1,0:T(8,128)S(1)}, f32[384,128]{1,0:T(8,128)S(1)}, u32[]{:S(2)}, u32[]{:S(2)}) collective-permute-start(f32[384,128]{1,0:T(8,128)S(1)} %add.31), channel_id=1, source_target_pairs={{0,8},{4,12},{8,0},{12,4},{1,9},{5,13},{9,1},{13,5},{2,10},{6,14},... | collective-permute-start | bytes 589832 | tf_op jit(solution)/shard_map/ppermute | solution.py:48
  20.3 8.1 %collective-permute-done.3 = f32[384,128]{1,0:T(8,128)S(1)} collective-permute-done((f32[384,128]{1,0:T(8,128)S(1)}, f32[384,128]{1,0:T(8,128)S(1)}, u32[]{:S(2)}, u32[]{:S(2)}) %collective-permute-start.3) | collective-permute-done | bytes 196640 | tf_op jit(solution)/shard_map/ppermute | solution.py:48
  29.1 2.9 %cholesky.74 = f32[32,32]{1,0:T(8,128)S(1)} custom-call(f32[32,32]{1,0:T(8,128)S(1)} %fusion.32), custom_call_target="Cholesky" | custom-call | tf_op jit(solution)/shard_map/jit(cholesky)/cholesky | solution.py:21
  32.7 0.7 fusion.21
  33.3 2.4 %custom-call.8 = f32[1,32,32]{1,2,0:T(8,128)S(1)} custom-call(f32[1,32,32]{2,1,0:T(8,128)S(1)} %fusion.21), custom_call_target="InvertDiagBlocksLowerTriangular" | custom-call | tf_op jit(solution)/shard_map/jit(_solve_triangular)/triangular_solve | solution.py:22
  36.6 2.9 %cholesky.85 = f32[32,32]{1,0:T(8,128)S(1)} custom-call(f32[32,32]{1,0:T(8,128)S(1)} %fusion.30), custom_call_target="Cholesky" | custom-call | tf_op jit(solution)/shard_map/jit(cholesky)/cholesky | solution.py:21
  40.2 0.7 fusion.22
  40.9 2.4 %custom-call.9 = f32[1,32,32]{1,2,0:T(8,128)S(1)} custom-call(f32[1,32,32]{2,1,0:T(8,128)S(1)} %fusion.22), custom_call_target="InvertDiagBlocksLowerTriangular" | custom-call | tf_op jit(solution)/shard_map/jit(_solve_triangular)/triangular_solve | solution.py:22
  44.1 2.9 %cholesky.96 = f32[32,32]{1,0:T(8,128)S(1)} custom-call(f32[32,32]{1,0:T(8,128)S(1)} %fusion.28), custom_call_target="Cholesky" | custom-call | tf_op jit(solution)/shard_map/jit(cholesky)/cholesky | solution.py:21
  47.7 0.7 fusion.23
  48.4 2.4 %custom-call.10 = f32[1,32,32]{1,2,0:T(8,128)S(1)} custom-call(f32[1,32,32]{2,1,0:T(8,128)S(1)} %fusion.23), custom_call_target="InvertDiagBlocksLowerTriangular" | custom-call | tf_op jit(solution)/shard_map/jit(_solve_triangular)/triangular_solve | solution.py:22
  51.7 2.9 %cholesky.107 = f32[32,32]{1,0:T(8,128)S(1)} custom-call(f32[32,32]{1,0:T(8,128)S(1)} %fusion.26), custom_call_target="Cholesky" | custom-call | tf_op jit(solution)/shard_map/jit(cholesky)/cholesky | solution.py:21
  55.3 0.7 fusion.24
  56.0 2.4 %custom-call.11 = f32[1,32,32]{1,2,0:T(8,128)S(1)} custom-call(f32[1,32,32]{2,1,0:T(8,128)S(1)} %fusion.24), custom_call_target="InvertDiagBlocksLowerTriangular" | custom-call | tf_op jit(solution)/shard_map/jit(_solve_triangular)/triangular_solve | solution.py:22
  58.9 1.5 %fusion.1 = bf16[256,1,640]{2,0,1:T(8,128)(2,1)S(1)} fusion(bf16[32,640]{1,0:T(8,128)(2,1)S(1)} %convolution_convert_fusion.1, bf16[32,256]{1,0:T(8,128)(2,1)S(1)} %convolution_convert_fusion.2, bf16[640,256]{1,0:T(8,128)(2,1)S(1)} %copy-done, s32[256]{0:T(256)S(1)} %iota_add_fusion, pred[256]{0:T(512)(128)(4,1)S(1)} %iota_compare_fusion.4), kind=kOutput, calls=%fused_computation.3 | convolution fusion | flops 96206848 | bytes 713984 | tf_op jit(solution)/shard_map/dot_general | solution.py:100
  60.9 0.8 %reduce.4 = bf16[256,640]{1,0:T(8,128)(2,1)S(1)} reduce(bf16[256,1,640]{2,0,1:T(8,128)(2,1)S(1)} %fusion.1, bf16[]{:T(256)} %broadcast.63), dimensions={1}, to_apply=%copy.20.reduce_sub_computation | reduce | bytes 655362 | tf_op jit(solution)/shard_map/broadcast_in_dim | solution.py:104
  61.8 16.0 %all_to_all.18 = bf16[8,2,10240]{2,1,0:T(2,128)(2,1)S(1)} all-to-all(bf16[8,2,10240]{2,1,0:T(2,128)(2,1)S(1)} %reshape.8), channel_id=1, replica_groups=mesh['groups'=2,'pix'=4,'sub'=2,'inner'=2] {'pix','sub'}, dimensions={0} | all-to-all | bytes 655360 | tf_op jit(solution)/shard_map/all_to_all | solution.py:103
  78.2 0.8 %copy.21 = bf16[32,8,640]{2,1,0:T(8,128)(2,1)} copy(bf16[32,8,640]{2,0,1:T(8,128)(2,1)S(1)} %bitcast.74) | data formatting | bytes 655360 | tf_op jit(solution)/shard_map/all_to_all | solution.py:103
  (47 shorter events, 7.9 us)
Async XLA Ops:
  1.4 1.6 %collective-permute-start = (f32[384,128]{1,0:T(8,128)S(1)}, f32[384,128]{1,0:T(8,128)S(1)}, u32[]{:S(2)}, u32[]{:S(2)}) collective-permute-start(f32[384,128]{1,0:T(8,128)S(1)} %pad_maximum_fusion), channel_id=1, source_target_pairs={{0,1},{1,0},{2,3},{3,2},{4,5},{5,4},{6,7},{7,6},{8,9},{9,8},{10,11... | collective-permute-start | bytes 589832 | tf_op jit(solution)/shard_map/ppermute | solution.py:48
  3.1 8.1 %collective-permute-start.1 = (f32[384,128]{1,0:T(8,128)S(1)}, f32[384,128]{1,0:T(8,128)S(1)}, u32[]{:S(2)}, u32[]{:S(2)}) collective-permute-start(f32[384,128]{1,0:T(8,128)S(1)} %fusion.44), channel_id=1, source_target_pairs={{0,2},{2,0},{1,3},{3,1},{4,6},{6,4},{5,7},{7,5},{8,10},{10,8},{9,1... | collective-permute-start | bytes 589832 | tf_op jit(solution)/shard_map/ppermute | solution.py:48
  11.2 6.4 %collective-permute-start.2 = (f32[384,128]{1,0:T(8,128)S(1)}, f32[384,128]{1,0:T(8,128)S(1)}, u32[]{:S(2)}, u32[]{:S(2)}) collective-permute-start(f32[384,128]{1,0:T(8,128)S(1)} %add.30), channel_id=1, source_target_pairs={{0,4},{4,0},{8,12},{12,8},{1,5},{5,1},{9,13},{13,9},{2,6},{6,2},{1... | collective-permute-start | bytes 589832 | tf_op jit(solution)/shard_map/ppermute | solution.py:48
  17.7 10.7 %collective-permute-start.3 = (f32[384,128]{1,0:T(8,128)S(1)}, f32[384,128]{1,0:T(8,128)S(1)}, u32[]{:S(2)}, u32[]{:S(2)}) collective-permute-start(f32[384,128]{1,0:T(8,128)S(1)} %add.31), channel_id=1, source_target_pairs={{0,8},{4,12},{8,0},{12,4},{1,9},{5,13},{9,1},{13,5},{2,10},{6,14},... | collective-permute-start | bytes 589832 | tf_op jit(solution)/shard_map/ppermute | solution.py:48
  51.1 7.6 %copy-start = (bf16[640,256]{1,0:T(8,128)(2,1)S(1)}, bf16[640,256]{1,0:T(8,128)(2,1)}, u32[]{:S(2)}) copy-start(bf16[640,256]{1,0:T(8,128)(2,1)} %param.4) | copy-start | bytes 983044
where the time goes:
time: 79.2 us; the launch traced here: 79 us
  other arithmetic  27.7 us (35%)
  waiting for transfers between devices  18.9 us (24%)
  blocking collectives  16 us (20%)
  starting transfers between devices  7.98 us (10%)
  matrix products  6.01 us (8%)
  local copies, waits for them, and re-layouts  2.2 us (3%)
    ppermute x4, waiting for transfers between devices, butterfly_sum(): x = x + lax.ppermute(x, name, [(i, i ^ d) for i in range(n)])  18.9 us
    all_to_all x1, blocking collectives, local(): lax.all_to_all(coefficients[:, None, :], ('pix', 'sub'), split_axis=0, co...  16 us
    another operation x12, other arithmetic, leading_modes(): lower_factor = jnp.linalg.cholesky(cross_gram)  14.4 us
    another operation x8, other arithmetic, leading_modes(): jax.scipy.linalg.solve_triangular(lower_factor, product.T, lower=True)  12.3 us
    ppermute x4, starting transfers between devices, butterfly_sum(): x = x + lax.ppermute(x, name, [(i, i ^ d) for i in range(n)])  7.98 us
    dot_general x8, matrix products, matmul_high(): return jnp.dot(left, right, precision=lax.Precision.HIGHEST)  1.94 us
  transfers between devices with their start and end apart: 4, of which 4 were waited for; matrix products, arithmetic and copies ran while one was open for 0% of the time, Pallas kernels for 0%

commit v1 on v0

--- a/solution.py
+++ b/solution.py
@@ -7,6 +7,13 @@
 MODES = 32
 ITERS = 4
 VARIANT = "symbutterfly"
+
+
+def stacked_exchange(block, axis, split, join):
+    devices = lax.axis_size(axis)
+    blocks = jnp.stack(jnp.split(block, devices, axis=split), axis=0)
+    blocks = lax.all_to_all(blocks, axis, split_axis=0, concat_axis=0)
+    return jnp.concatenate(blocks, axis=join)
 
 
 def matmul_high(left, right):
@@ -100,9 +107,7 @@
         coefficients = lax.dot_general(
             table_b, cleaned, (((1,), (1,)), ((), ())), preferred_element_type=jnp.float32
         ).astype(jnp.bfloat16)
-        spectra = lax.all_to_all(
-            coefficients[:, None, :], ("pix", "sub"), split_axis=0, concat_axis=1, tiled=True
-        )
+        spectra = stacked_exchange(coefficients[:, None, :], ("pix", "sub"), 0, 1)
         return spectra
 
     return local

time: 79.2 us -> 77.5 us (0.979)
  local copies, waits for them, and re-layouts: 2.2 us -> 1.33 us
  other arithmetic: 27.7 us -> 26.9 us
    all_to_all x1 -> x0, local copies, waits for them, and re-layouts: 0.83 us -> none  [local(): lax.all_to_all(coefficients[:, None, :], ('pix', 'sub'), split_axis=0, co...]
    reshape x0 -> x1, local copies, waits for them, and re-layouts: none -> 0.83 us  [stacked_exchange(): return jnp.concatenate(blocks, axis=join)]
    broadcast_in_dim x1 -> x0, other arithmetic: 0.82 us -> none  [local(): coefficients[:, None, :]]
where the time goes in v1:
time: 77.5 us; the launch traced here: 77.3 us
  other arithmetic  26.9 us (35%)
  waiting for transfers between devices  18.9 us (24%)
  blocking collectives  16 us (21%)
  starting transfers between devices  7.98 us (10%)
  matrix products  6.01 us (8%)
  local copies, waits for them, and re-layouts  1.33 us (2%)
    ppermute x4, waiting for transfers between devices, butterfly_sum(): x = x + lax.ppermute(x, name, [(i, i ^ d) for i in range(n)])  18.9 us
    all_to_all x1, blocking collectives, stacked_exchange(): blocks = lax.all_to_all(blocks, axis, split_axis=0, concat_axis=0)  16 us
    another operation x12, other arithmetic, leading_modes(): lower_factor = jnp.linalg.cholesky(cross_gram)  14.4 us
    another operation x8, other arithmetic, leading_modes(): jax.scipy.linalg.solve_triangular(lower_factor, product.T, lower=True)  12.3 us
    ppermute x4, starting transfers between devices, butterfly_sum(): x = x + lax.ppermute(x, name, [(i, i ^ d) for i in range(n)])  7.98 us
    dot_general x8, matrix products, matmul_high(): return jnp.dot(left, right, precision=lax.Precision.HIGHEST)  1.94 us
  transfers between devices with their start and end apart: 4, of which 4 were waited for; matrix products, arithmetic and copies ran while one was open for 0% of the time, Pallas kernels for 0%

profile of v1, /device:TPU:0, one launch (start us, length us, event | category | flops | bytes accessed | tf_op | source)
XLA Modules:
  0.0 77.3 jit_solution(16545306248271003670)
XLA Ops:
  0.0 1.4 %fusion.56 = f32[256,256]{1,0:T(8,128)S(1)} fusion(bf16[640,256]{1,0:T(8,128)(2,1)} %param.4), kind=kOutput, calls=%fused_computation.93 | convolution fusion | flops 83886080 | bytes 589824 | tf_op jit(solution)/shard_map/dot_general | solution.py:95
  2.0 1.1 %collective-permute-done = f32[384,128]{1,0:T(8,128)S(1)} collective-permute-done((f32[384,128]{1,0:T(8,128)S(1)}, f32[384,128]{1,0:T(8,128)S(1)}, u32[]{:S(2)}, u32[]{:S(2)}) %collective-permute-start) | collective-permute-done | bytes 196640 | tf_op jit(solution)/shard_map/ppermute | solution.py:55
  3.1 2.9 %collective-permute-start.1 = (f32[384,128]{1,0:T(8,128)S(1)}, f32[384,128]{1,0:T(8,128)S(1)}, u32[]{:S(2)}, u32[]{:S(2)}) collective-permute-start(f32[384,128]{1,0:T(8,128)S(1)} %fusion.51), channel_id=1, source_target_pairs={{0,2},{2,0},{1,3},{3,1},{4,6},{6,4},{5,7},{7,5},{8,10},{10,8},{9,1... | collective-permute-start | bytes 589832 | tf_op jit(solution)/shard_map/ppermute | solution.py:55
  6.0 5.2 %collective-permute-done.1 = f32[384,128]{1,0:T(8,128)S(1)} collective-permute-done((f32[384,128]{1,0:T(8,128)S(1)}, f32[384,128]{1,0:T(8,128)S(1)}, u32[]{:S(2)}, u32[]{:S(2)}) %collective-permute-start.1) | collective-permute-done | bytes 196640 | tf_op jit(solution)/shard_map/ppermute | solution.py:55
  11.2 1.9 %collective-permute-start.2 = (f32[384,128]{1,0:T(8,128)S(1)}, f32[384,128]{1,0:T(8,128)S(1)}, u32[]{:S(2)}, u32[]{:S(2)}) collective-permute-start(f32[384,128]{1,0:T(8,128)S(1)} %add.30), channel_id=1, source_target_pairs={{0,4},{4,0},{8,12},{12,8},{1,5},{5,1},{9,13},{13,9},{2,6},{6,2},{1... | collective-permute-start | bytes 589832 | tf_op jit(solution)/shard_map/ppermute | solution.py:55
  13.1 4.5 %collective-permute-done.2 = f32[384,128]{1,0:T(8,128)S(1)} collective-permute-done((f32[384,128]{1,0:T(8,128)S(1)}, f32[384,128]{1,0:T(8,128)S(1)}, u32[]{:S(2)}, u32[]{:S(2)}) %collective-permute-start.2) | collective-permute-done | bytes 196640 | tf_op jit(solution)/shard_map/ppermute | solution.py:55
  17.7 2.6 %collective-permute-start.3 = (f32[384,128]{1,0:T(8,128)S(1)}, f32[384,128]{1,0:T(8,128)S(1)}, u32[]{:S(2)}, u32[]{:S(2)}) collective-permute-start(f32[384,128]{1,0:T(8,128)S(1)} %add.31), channel_id=1, source_target_pairs={{0,8},{4,12},{8,0},{12,4},{1,9},{5,13},{9,1},{13,5},{2,10},{6,14},... | collective-permute-start | bytes 589832 | tf_op jit(solution)/shard_map/ppermute | solution.py:55
  20.3 8.1 %collective-permute-done.3 = f32[384,128]{1,0:T(8,128)S(1)} collective-permute-done((f32[384,128]{1,0:T(8,128)S(1)}, f32[384,128]{1,0:T(8,128)S(1)}, u32[]{:S(2)}, u32[]{:S(2)}) %collective-permute-start.3) | collective-permute-done | bytes 196640 | tf_op jit(solution)/shard_map/ppermute | solution.py:55
  29.1 2.9 %cholesky.74 = f32[32,32]{1,0:T(8,128)S(1)} custom-call(f32[32,32]{1,0:T(8,128)S(1)} %fusion.39), custom_call_target="Cholesky" | custom-call | tf_op jit(solution)/shard_map/jit(cholesky)/cholesky | solution.py:28
  32.7 0.7 fusion.28
  33.3 2.4 %custom-call.8 = f32[1,32,32]{1,2,0:T(8,128)S(1)} custom-call(f32[1,32,32]{2,1,0:T(8,128)S(1)} %fusion.28), custom_call_target="InvertDiagBlocksLowerTriangular" | custom-call | tf_op jit(solution)/shard_map/jit(_solve_triangular)/triangular_solve | solution.py:29
  36.6 2.9 %cholesky.85 = f32[32,32]{1,0:T(8,128)S(1)} custom-call(f32[32,32]{1,0:T(8,128)S(1)} %fusion.37), custom_call_target="Cholesky" | custom-call | tf_op jit(solution)/shard_map/jit(cholesky)/cholesky | solution.py:28
  40.2 0.7 fusion.29
  40.9 2.4 %custom-call.9 = f32[1,32,32]{1,2,0:T(8,128)S(1)} custom-call(f32[1,32,32]{2,1,0:T(8,128)S(1)} %fusion.29), custom_call_target="InvertDiagBlocksLowerTriangular" | custom-call | tf_op jit(solution)/shard_map/jit(_solve_triangular)/triangular_solve | solution.py:29
  44.1 2.9 %cholesky.96 = f32[32,32]{1,0:T(8,128)S(1)} custom-call(f32[32,32]{1,0:T(8,128)S(1)} %fusion.35), custom_call_target="Cholesky" | custom-call | tf_op jit(solution)/shard_map/jit(cholesky)/cholesky | solution.py:28
  47.1 0.6 compare_reduce_fusion.1
  47.7 0.7 fusion.30
  48.4 2.4 %custom-call.10 = f32[1,32,32]{1,2,0:T(8,128)S(1)} custom-call(f32[1,32,32]{2,1,0:T(8,128)S(1)} %fusion.30), custom_call_target="InvertDiagBlocksLowerTriangular" | custom-call | tf_op jit(solution)/shard_map/jit(_solve_triangular)/triangular_solve | solution.py:29
  51.7 2.9 %cholesky.107 = f32[32,32]{1,0:T(8,128)S(1)} custom-call(f32[32,32]{1,0:T(8,128)S(1)} %fusion.33), custom_call_target="Cholesky" | custom-call | tf_op jit(solution)/shard_map/jit(cholesky)/cholesky | solution.py:28
  55.3 0.7 fusion.31
  56.0 2.4 %custom-call.11 = f32[1,32,32]{1,2,0:T(8,128)S(1)} custom-call(f32[1,32,32]{2,1,0:T(8,128)S(1)} %fusion.31), custom_call_target="InvertDiagBlocksLowerTriangular" | custom-call | tf_op jit(solution)/shard_map/jit(_solve_triangular)/triangular_solve | solution.py:29
  58.9 1.5 %convolution_convert_fusion = bf16[256,640]{1,0:T(8,128)(2,1)S(1)} fusion(bf16[32,640]{1,0:T(8,128)(2,1)S(1)} %convolution_convert_fusion.1, bf16[32,256]{1,0:T(8,128)(2,1)S(1)} %convolution_convert_fusion.2, bf16[640,256]{1,0:T(8,128)(2,1)S(1)} %copy-done, s32[256]{0:T(256)S(1)} %iota_add_fusion, pred[256]{0:T(512)(128)(4,1)S(1)} %iota_compare_fusion.4), kind=kOutput, calls=%fused_computation.1 | convolution fusion | flops 96206848 | bytes 713984 | tf_op jit(solution)/shard_map/dot_general | solution.py:107
  60.5 16.0 %all_to_all.5 = bf16[8,32,1,640]{3,1,2,0:T(8,128)(2,1)S(1)} all-to-all(bf16[8,32,1,640]{3,1,2,0:T(8,128)(2,1)S(1)} %fusion.13), channel_id=1, replica_groups=mesh['groups'=2,'pix'=4,'sub'=2,'inner'=2] {'pix','sub'}, dimensions={0} | all-to-all | bytes 655360 | tf_op jit(solution)/shard_map/all_to_all | solution.py:15
  76.5 0.8 %copy.7 = bf16[32,8,640]{2,1,0:T(8,128)(2,1)} copy(bf16[32,8,640]{2,0,1:T(8,128)(2,1)S(1)} %bitcast.102) | data formatting | bytes 655360 | tf_op jit(solution)/shard_map/reshape | solution.py:16
  (50 shorter events, 6.4 us)
Async XLA Ops:
  1.4 1.6 %collective-permute-start = (f32[384,128]{1,0:T(8,128)S(1)}, f32[384,128]{1,0:T(8,128)S(1)}, u32[]{:S(2)}, u32[]{:S(2)}) collective-permute-start(f32[384,128]{1,0:T(8,128)S(1)} %pad_maximum_fusion), channel_id=1, source_target_pairs={{0,1},{1,0},{2,3},{3,2},{4,5},{5,4},{6,7},{7,6},{8,9},{9,8},{10,11... | collective-permute-start | bytes 589832 | tf_op jit(solution)/shard_map/ppermute | solution.py:55
  3.1 8.1 %collective-permute-start.1 = (f32[384,128]{1,0:T(8,128)S(1)}, f32[384,128]{1,0:T(8,128)S(1)}, u32[]{:S(2)}, u32[]{:S(2)}) collective-permute-start(f32[384,128]{1,0:T(8,128)S(1)} %fusion.51), channel_id=1, source_target_pairs={{0,2},{2,0},{1,3},{3,1},{4,6},{6,4},{5,7},{7,5},{8,10},{10,8},{9,1... | collective-permute-start | bytes 589832 | tf_op jit(solution)/shard_map/ppermute | solution.py:55
  11.2 6.4 %collective-permute-start.2 = (f32[384,128]{1,0:T(8,128)S(1)}, f32[384,128]{1,0:T(8,128)S(1)}, u32[]{:S(2)}, u32[]{:S(2)}) collective-permute-start(f32[384,128]{1,0:T(8,128)S(1)} %add.30), channel_id=1, source_target_pairs={{0,4},{4,0},{8,12},{12,8},{1,5},{5,1},{9,13},{13,9},{2,6},{6,2},{1... | collective-permute-start | bytes 589832 | tf_op jit(solution)/shard_map/ppermute | solution.py:55
  17.7 10.7 %collective-permute-start.3 = (f32[384,128]{1,0:T(8,128)S(1)}, f32[384,128]{1,0:T(8,128)S(1)}, u32[]{:S(2)}, u32[]{:S(2)}) collective-permute-start(f32[384,128]{1,0:T(8,128)S(1)} %add.31), channel_id=1, source_target_pairs={{0,8},{4,12},{8,0},{12,4},{1,9},{5,13},{9,1},{13,5},{2,10},{6,14},... | collective-permute-start | bytes 589832 | tf_op jit(solution)/shard_map/ppermute | solution.py:55
  51.1 7.6 %copy-start = (bf16[640,256]{1,0:T(8,128)(2,1)S(1)}, bf16[640,256]{1,0:T(8,128)(2,1)}, u32[]{:S(2)}) copy-start(bf16[640,256]{1,0:T(8,128)(2,1)} %param.4) | copy-start | bytes 983044
